TPU v7x, 32 devices: a whole 2x2x4 slice. The times are simulated.
32 devices in a mesh: dp: 2 (over x), seq: 16 (over z, y, core).
Axes of the slice: x: 2, y: 2, z: 4, core: 2. Of those that a mesh axis runs over, the one named last changes fastest.
Arguments:
- frames: bfloat16 [2, 16, 64, 48, 128], P('dp', None, 'seq'), may hold values from -6 to 6
- frame_counts: int32 [2, 4], P('dp'), may hold values from 1 to 12, 16 in all within a row
- clip_group: int32 [2, 4], P('dp'), may hold values 0 or 1
- timesteps: int32 [2, 4], P('dp'), may hold values from 0 to 999
- owner_map: int32 [2, 16, 192, 1], P('dp', 'seq'), may hold values from 0 to 15; in each aligned block of 192 rows (0 to 191, 192 to 383, ..., all dimensions but the last counted through in order) at most 18 rows name the same one
- conv_weight: bfloat16 [3, 3, 3, 128, 128], replicated, may hold values from -0.109375 to 0.109375
- w_latent: bfloat16 [2048, 64], replicated, may hold values from -0.125 to 0.125
- hidden: bfloat16 [2, 4608, 3072], P('dp', 'seq'), may hold values from -6 to 6
- noise: float32 [2, 4608, 64], P('dp', 'seq'), may hold values from -6 to 6
- teacher: float32 [2, 4608, 64], P('dp', 'seq'), may hold values from -6 to 6
- w_out: bfloat16 [3072, 64], replicated, may hold values from -0.109375 to 0.109375
Outputs:
- latent: bfloat16 [2, 16, 16, 768], P('dp', None, 'seq')
- clip_loss: float32 [2, 4], P('dp')
- grad_out: float32 [3072, 64], P('seq')
Inputs may be any that keep to these rules, and one draw needn't show every extreme that they name: `owner_map`: among the tokens of one device no owner is named more than 18 times, a bound that some block reaches. `frame_counts`: the counts of a group sum to 16; the largest is exactly 12.
All inputs are finite; a program needn't handle non-finite values. No bound on the sum of `clip_group` on one device may be relied on, other than what follows from the above.
Results may differ from a plain program's by a relative error of at most 0.0055.
Values may be sent and summed in bfloat16 or wider, within the bound.
No kernel may reach another device: no remote copies, remote signals or barrier semaphores. Data moves between devices by JAX's collectives and lax.ppermute only.
A program may use at most 64 MiB of HBM per device.

v0:
```python
import jax
import jax.numpy as jnp
from jax import lax
from jax.sharding import PartitionSpec as P

LAT = 64
CLIPS = 4


def with_halo(cells, sides, width):
    for axis, dim in sides:
        count = lax.axis_size(axis)
        ends = count - 1
        head = lax.slice_in_dim(cells, 0, width, axis=dim)
        tail = lax.slice_in_dim(cells, cells.shape[dim] - width, cells.shape[dim], axis=dim)
        cells = jnp.concatenate(
            [
                lax.ppermute(tail, axis, [(i, (i + 1) % count) for i in range(ends)]),
                cells,
                lax.ppermute(head, axis, [((i + 1) % count, i) for i in range(ends)]),
            ],
            axis=dim,
        )
    return cells


def conv_rows(padded, kernel, keep, first, count):
    nframes = keep.shape[1]
    width = padded.shape[2] - 2
    chans = padded.shape[3]
    total = jnp.zeros((nframes, count * width, chans), jnp.float32)
    for lag in range(3):
        pieces = [
            padded[2 - lag : 2 - lag + nframes, first + i : first + i + count, j : j + width, :]
            for i in range(3)
            for j in range(3)
        ]
        columns = jnp.concatenate(pieces, axis=-1).reshape(-1, 9 * chans)
        part = jnp.dot(
            columns, kernel[lag].reshape(9 * chans, chans), preferred_element_type=jnp.float32
        )
        total = total + part.reshape(nframes, count * width, chans) * keep[lag][:, None, None]
    return total.reshape(nframes, count, width, chans)


def per_device(
    frames,
    frame_counts,
    clip_group,
    timesteps,
    owner_map,
    conv_weight,
    w_latent,
    hidden,
    noise,
    teacher,
    w_out,
):
    nseq = lax.axis_size("seq")
    local = frames[0]
    nframes, nrows, width, chans = local.shape
    tok_rows = nrows // 4
    tok_cols = width // 4
    per_frame = nrows * nseq // 4 * tok_cols
    counts = frame_counts[0]
    ends = jnp.cumsum(counts)
    index = jnp.arange(nframes, dtype=jnp.int32)
    clip_of = jnp.sum((index[:, None] >= ends[None, :]).astype(jnp.int32), axis=1)
    clip_hot = (clip_of[:, None] == jnp.arange(CLIPS, dtype=jnp.int32)[None, :]).astype(jnp.int32)
    starts = jnp.sum(clip_hot * (ends - counts)[None, :], axis=1)
    keep = jnp.stack([(index - lag >= starts).astype(jnp.float32) for lag in range(3)])
    rimmed = with_halo(frames, (("seq", 2),), 1)[0]
    outer_pad = jnp.pad(rimmed, ((2, 0), (0, 0), (1, 1), (0, 0)))
    conv = conv_rows(outer_pad, conv_weight, keep, 0, nrows)
    cells = (local.astype(jnp.float32) + jax.nn.silu(conv)).astype(jnp.bfloat16)
    patches = (
        cells.reshape(nframes, tok_rows, 4, tok_cols, 4, chans)
        .transpose(0, 1, 3, 2, 4, 5)
        .reshape(-1, 16 * chans)
    )
    tokens = jnp.dot(patches, w_latent, preferred_element_type=jnp.float32).astype(jnp.bfloat16)
    latent_out = tokens.reshape(1, nframes, tok_rows, tok_cols * LAT)
    slots = hidden.shape[1]
    capacity = slots // nseq
    owners = owner_map.reshape(-1)
    owner_hot = (owners[:, None] == jnp.arange(nseq, dtype=jnp.int32)[None, :]).astype(jnp.int32)
    rank = jnp.sum(jnp.cumsum(owner_hot, axis=0) * owner_hot, axis=1) - 1
    dest = owners * capacity + rank
    select = (dest[None, :] == jnp.arange(slots, dtype=jnp.int32)[:, None]).astype(jnp.bfloat16)
    tok_clip = jnp.repeat(clip_of, tok_rows * tok_cols).astype(jnp.float32) + 1.0
    outgoing = (
        jnp.dot(select, tokens, preferred_element_type=jnp.float32)
        .astype(jnp.bfloat16)
        .reshape(nseq, capacity, LAT)
    )
    labels = (
        jnp.dot(select, tok_clip.astype(jnp.bfloat16)[:, None], preferred_element_type=jnp.float32)
        .astype(jnp.bfloat16)
        .reshape(nseq, capacity)
    )
    arrived, arrived_tags = (
        lax.all_to_all(outgoing, "seq", split_axis=0, concat_axis=0, tiled=True),
        lax.all_to_all(labels, "seq", split_axis=0, concat_axis=0, tiled=True),
    )
    x0 = arrived.reshape(slots, LAT).astype(jnp.float32)
    tag = arrived_tags.reshape(slots).astype(jnp.float32)
    kind = clip_group[0].astype(jnp.float32)
    coef = (
        (2.0 * kind - 1.0)
        * (0.1 + timesteps[0].astype(jnp.float32) / 1000.0)
        / (counts.astype(jnp.float32) * per_frame)
    )
    slot_hot = (tag[:, None] == (jnp.arange(CLIPS, dtype=jnp.float32) + 1.0)[None, :]).astype(
        jnp.float32
    )
    slot_coef = jnp.sum(slot_hot * coef[None, :], axis=1)
    slot_kind = jnp.sum(slot_hot * kind[None, :], axis=1)
    states = hidden[0].astype(jnp.float32)
    mean = jnp.mean(states, axis=1, keepdims=True)
    centred = states - mean
    var = jnp.mean(centred * centred, axis=1, keepdims=True)
    normed = (centred * lax.rsqrt(var + 1e-06)).astype(jnp.bfloat16)
    pred = jnp.dot(normed, w_out, preferred_element_type=jnp.float32)
    target = slot_kind[:, None] * teacher[0] + (1.0 - slot_kind[:, None]) * (noise[0] - x0)
    diff = pred - target
    err = jnp.sum(diff * diff, axis=1)
    partial_loss = coef * jnp.sum(slot_hot * err[:, None], axis=0)
    clip_loss = lax.psum(partial_loss, "seq").reshape(1, CLIPS)
    dpred = (2.0 * slot_coef[:, None] * diff).astype(jnp.bfloat16)
    share_rows = normed.shape[1] // nseq
    grad_part = lax.dot_general(
        normed, dpred, (((0,), (0,)), ((), ())), preferred_element_type=jnp.float32
    )
    summed = lax.psum(grad_part, ("dp", "seq"))
    grad_mine = lax.dynamic_slice_in_dim(summed, lax.axis_index("seq") * share_rows, share_rows, 0)
    return (latent_out, clip_loss, grad_mine)


def solution(mesh):
    return jax.shard_map(
        per_device,
        mesh=mesh,
        in_specs=(
            P("dp", None, "seq", None, None),
            P("dp", None),
            P("dp", None),
            P("dp", None),
            P("dp", "seq", None, None),
            P(),
            P(),
            P("dp", "seq", None),
            P("dp", "seq", None),
            P("dp", "seq", None),
            P(),
        ),
        out_specs=(P("dp", None, "seq", None), P("dp", None), P("seq", None)),
        check_vma=False,
    )
```

profile of v0, /device:TPU:0, one launch (start us, length us, event | category | flops | bytes accessed | tf_op | source)
XLA Modules:
  0.0 210.9 jit_solution(1002889426171956777)
XLA Ops:
  7.2 2.0 fusion.43
  9.1 3.1 %collective-permute-start = (bf16[1,16,1,48,128]{4,3,2,1,0:T(8,128)(2,1)}, bf16[1,16,1,48,128]{4,3,2,1,0:T(8,128)(2,1)}, u32[]{:S(2)}, u32[]{:S(2)}) collective-permute-start(bf16[1,16,1,48,128]{4,3,2,1,0:T(8,128)(2,1)} %get-tuple-element.17), channel_id=1, source_target_pairs={{0,1},{1,2},{2,3},{3,4},{4,5},{5,6},{6,7},{7,8},{8,9},{9,10},{10,1... | collective-permute-start | bytes 589832 | tf_op jit(solution)/shard_map/ppermute | solution.py:18
  12.2 1.3 collective-permute-start.1
  13.5 0.8 reduce-window.10
  18.5 8.6 %all-to-all-start = ((bf16[16,1,18]{2,1,0:T(2,128)(2,1)}), bf16[16,1,18]{2,1,0:T(2,128)(2,1)S(1)}, u32[]{:S(2)}, u32[]{:S(2)}) async-start(bf16[16,1,18]{2,1,0:T(2,128)(2,1)} %all_to_all.12), calls=%async_computation | async-start | bytes 16384 | tf_op jit(solution)/shard_map/all_to_all | solution.py:103
  27.1 0.8 fusion.40
  27.9 1.9 fusion.42
  30.5 1.2 convert_bitcast_fusion.2
  34.6 1.6 copy.40
  36.3 0.8 fusion.37
  37.1 1.2 maximum_bitcast_fusion
  40.9 1.0 fusion.28
  46.3 2.2 %fusion.45 = f32[16,192,128]{2,1,0:T(8,128)S(1)} fusion(bf16[16,192,1152]{2,1,0:T(8,128)(2,1)S(1)} %bitcast.85, bf16[1152,128,1]{1,0,2:T(8,128)(2,1)S(1)} %bitcast.90), kind=kOutput, calls=%fused_computation.117 | convolution fusion | flops 905969664 | bytes 8945664 | tf_op jit(solution)/shard_map/dot_general | solution.py:39
  48.6 2.0 fusion.44
  50.6 2.1 %multiply_add_fusion = f32[16,192,128]{2,1,0:T(8,128)S(1)} fusion(f32[16,192,128]{2,1,0:T(8,128)S(1)} %fusion.45, f32[16,192,128]{2,1,0:T(8,128)S(1)} %fusion.44, bf16[16,192,1152]{2,1,0:T(8,128)(2,1)S(1)} %bitcast.84, bf16[1152,128,1]{1,0,2:T(8,128)(2,1)S(1)} %bitcast.91, f32[16]{0:T(128)S(1)} %copy-done.10, f32[16]{0:T(128)S(1)} %copy-done.11, ...), kind=kOutput, calls=%fused_computation.8 | convolution fusion | flops 907935744 | bytes 12091584 | tf_op jit(solution)/shard_map/dot_general | solution.py:39
  52.8 0.9 copy.41
  55.0 1.5 reshape.209
  56.5 1.5 convolution_convert_fusion.1
  59.1 6.0 %all-to-all-start.1 = ((bf16[16,2,576]{2,1,0:T(2,128)(2,1)}), bf16[16,2,576]{2,1,0:T(2,128)(2,1)S(1)}, u32[]{:S(2)}, u32[]{:S(2)}) async-start(bf16[16,2,576]{2,1,0:T(2,128)(2,1)} %reshape.236), calls=%async_computation.1 | async-start | bytes 81920 | tf_op jit(solution)/shard_map/all_to_all | solution.py:102
  65.2 6.6 %all-to-all-done.1 = bf16[16,2,576]{2,1,0:T(2,128)(2,1)S(1)} async-done(((bf16[16,2,576]{2,1,0:T(2,128)(2,1)}), bf16[16,2,576]{2,1,0:T(2,128)(2,1)S(1)}, u32[]{:S(2)}, u32[]{:S(2)}) %all-to-all-start.1) | async-done | bytes 36896 | tf_op jit(solution)/shard_map/all_to_all | solution.py:102
  73.1 1.4 fusion.34
  75.4 30.2 %psum.14 = f32[1,4]{1,0:T(1,128)} all-reduce(f32[1,4]{1,0:T(1,128)S(1)} %multiply_bitcast_fusion), channel_id=1, replica_groups=mesh['dp'=2,'seq'=16] {'seq'}, use_global_device_ids=true, to_apply=%region_11.12 | all-reduce | flops 4 | bytes 32 | tf_op jit(solution)/shard_map/psum | solution.py:128
  105.5 96.9 %all-reduce.4.cloned.1.call-done = f32[3072,64]{0,1:T(8,128)} async-done(((f32[3072,64]{0,1:T(8,128)}), f32[3072,64]{0,1:T(8,128)}) %all-reduce.4.cloned.1.call-update) | async-done | bytes 786448 | tf_op jit(solution)/shard_map/psum | solution.py:134
  202.4 1.6 constant_dynamic-slice_fusion
  (106 shorter events, 19.1 us)
Async XLA Ops:
  7.2 64.9 %copy-start = (bf16[3072,64]{0,1:T(8,128)(2,1)S(1)}, bf16[3072,64]{0,1:T(8,128)(2,1)}, u32[]{:S(2)}) copy-start(bf16[3072,64]{0,1:T(8,128)(2,1)} %param.21) | copy-start | bytes 1179652
  7.2 24.6 %copy-start.1 = (bf16[1,288,3072]{2,1,0:T(8,128)(2,1)S(1)}, bf16[1,288,3072]{2,1,0:T(8,128)(2,1)}, u32[]{:S(2)}) copy-start(bf16[1,288,3072]{2,1,0:T(8,128)(2,1)} %param.18) | copy-start | bytes 5308420
  9.1 27.9 %collective-permute-start = (bf16[1,16,1,48,128]{4,3,2,1,0:T(8,128)(2,1)}, bf16[1,16,1,48,128]{4,3,2,1,0:T(8,128)(2,1)}, u32[]{:S(2)}, u32[]{:S(2)}) collective-permute-start(bf16[1,16,1,48,128]{4,3,2,1,0:T(8,128)(2,1)} %get-tuple-element.17), channel_id=1, source_target_pairs={{0,1},{1,2},{2,3},{3,4},{4,5},{5,6},{6,7},{7,8},{8,9},{9,10},{10,1... | collective-permute-start | bytes 589832 | tf_op jit(solution)/shard_map/ppermute | solution.py:18
  12.2 24.9 %collective-permute-start.1 = (bf16[1,16,1,48,128]{4,3,2,1,0:T(8,128)(2,1)}, bf16[1,16,1,48,128]{4,3,2,1,0:T(8,128)(2,1)}, u32[]{:S(2)}, u32[]{:S(2)}) collective-permute-start(bf16[1,16,1,48,128]{4,3,2,1,0:T(8,128)(2,1)} %get-tuple-element.18), channel_id=1, source_target_pairs={{1,0},{2,1},{3,2},{4,3},{5,4},{6,5},{7,6},{8,7},{9,8},{10,9},{11,1... | collective-permute-start | bytes 589832 | tf_op jit(solution)/shard_map/ppermute | solution.py:20
  17.4 1.1 copy-start.14
  18.5 17.7 %all-to-all-start = ((bf16[16,1,18]{2,1,0:T(2,128)(2,1)}), bf16[16,1,18]{2,1,0:T(2,128)(2,1)S(1)}, u32[]{:S(2)}, u32[]{:S(2)}) async-start(bf16[16,1,18]{2,1,0:T(2,128)(2,1)} %all_to_all.12), calls=%async_computation | async-start | bytes 16384 | tf_op jit(solution)/shard_map/all_to_all | solution.py:103
  27.1 5.6 %copy-start.2 = (bf16[1,288,3072]{2,1,0:T(8,128)(2,1)S(1)}, bf16[1,288,3072]{2,1,0:T(8,128)(2,1)}, u32[]{:S(2)}) copy-start(bf16[1,288,3072]{2,1,0:T(8,128)(2,1)} %param.18) | copy-start | bytes 5308420
  31.8 1.7 copy-start.16
  31.8 1.7 copy-start.17
  31.8 1.7 copy-start.18
  31.8 2.8 %copy-start.4 = (bf16[1,16,4,48,128]{4,3,2,1,0:T(8,128)(2,1)S(1)}, bf16[1,16,4,48,128]{4,3,2,1,0:T(8,128)(2,1)}, u32[]{:S(2)}) copy-start(bf16[1,16,4,48,128]{4,3,2,1,0:T(8,128)(2,1)} %param.11) | copy-start | bytes 2359300
  48.5 2.1 copy-start.5
  48.5 2.1 copy-start.9
  48.5 2.1 copy-start.10
  48.6 2.1 copy-start.11
  52.8 1.4 copy-start.3
  54.2 2.3 %copy-start.6 = (bf16[2048,64]{0,1:T(8,128)(2,1)S(1)}, bf16[2048,64]{0,1:T(8,128)(2,1)}, u32[]{:S(2)}) copy-start(bf16[2048,64]{0,1:T(8,128)(2,1)} %param.17) | copy-start | bytes 786436
  54.2 3.8 %copy-start.15 = (s32[192]{0:T(256)S(1)}, s32[192]{0:T(256)}, u32[]{:S(2)}) copy-start(s32[192]{0:T(256)} %copy-done.14) | copy-start | bytes 2308
  54.6 17.5 %copy-start.7 = (f32[1,288,64]{1,2,0:T(8,128)S(1)}, f32[1,288,64]{1,2,0:T(8,128)}, u32[]{:S(2)}) copy-start(f32[1,288,64]{1,2,0:T(8,128)} %param.19) | copy-start | bytes 221188
  54.6 17.5 %copy-start.8 = (f32[1,288,64]{1,2,0:T(8,128)S(1)}, f32[1,288,64]{1,2,0:T(8,128)}, u32[]{:S(2)}) copy-start(f32[1,288,64]{1,2,0:T(8,128)} %param.20) | copy-start | bytes 221188
  56.5 16.4 %copy-start.12 = (f32[4]{0:T(128)S(1)}, f32[4]{0:T(128)}, u32[]{:S(2)}) copy-start(f32[4]{0:T(128)} %iota_add_fusion) | copy-start | bytes 52
  56.5 16.4 %copy-start.13 = (f32[4]{0:T(128)S(1)}, f32[4]{0:T(128)}, u32[]{:S(2)}) copy-start(f32[4]{0:T(128)} %fusion.41) | copy-start | bytes 52
  59.1 12.7 %all-to-all-start.1 = ((bf16[16,2,576]{2,1,0:T(2,128)(2,1)}), bf16[16,2,576]{2,1,0:T(2,128)(2,1)S(1)}, u32[]{:S(2)}, u32[]{:S(2)}) async-start(bf16[16,2,576]{2,1,0:T(2,128)(2,1)} %reshape.236), calls=%async_computation.1 | async-start | bytes 81920 | tf_op jit(solution)/shard_map/all_to_all | solution.py:102
  65.1 137.3 %all-reduce.4.cloned.1.call-start = ((), (), s32[]{:S(2)}) async-start(), calls=%async_computation.2 | async-start | bytes 1572864 | tf_op jit(solution)/shard_map/psum | solution.py:134
Sparse Core Ops, SparseCore 0:
  74.7 127.7 all-reduce.3
where the time goes:
time: 211 us
  waiting for transfers between devices  104 us (49%)
  blocking collectives  30.2 us (14%)
  local copies, waits for them, and re-layouts  21.4 us (10%)
  starting transfers between devices  19 us (9%)
  between operations  14.6 us (7%)
  other arithmetic  11.7 us (6%)
  matrix products  10.4 us (5%)
    psum x1, waiting for transfers between devices, per_device(): summed = lax.psum(grad_part, ('dp', 'seq'))  96.9 us
    psum x1, blocking collectives, per_device(): clip_loss = lax.psum(partial_loss, 'seq').reshape(1, CLIPS)  30.2 us
    all_to_all x1, starting transfers between devices, per_device(): lax.all_to_all(labels, 'seq', split_axis=0, concat_axis=0, tiled=True)  8.62 us
    unnamed x59, local copies, waits for them, and re-layouts  7.35 us
    all_to_all x1, waiting for transfers between devices, per_device(): lax.all_to_all(outgoing, 'seq', split_axis=0, concat_axis=0, tiled=True)  6.64 us
    dot_general x3, matrix products, conv_rows(): jnp.dot(columns, kernel[lag].reshape(9 * chans, chans), preferred_element...  6.37 us
    all_to_all x1, starting transfers between devices, per_device(): lax.all_to_all(outgoing, 'seq', split_axis=0, concat_axis=0, tiled=True)  6.01 us
  transfers between devices with their start and end apart: 5, of which 2 were waited for; matrix products, arithmetic and copies ran while one was open for 7% of the time, Pallas kernels for 0%

commit v1 on v0

--- a/solution.py
+++ b/solution.py
@@ -5,6 +5,29 @@
 
 LAT = 64
 CLIPS = 4
+
+
+def cut_along(array, dim, devices):
+    before, after = (array.shape[:dim], array.shape[dim + 1 :])
+    return jnp.moveaxis(array.reshape(*before, devices, -1, *after), dim, 0)
+
+
+def in_order(tiles, dim):
+    tiles = jnp.moveaxis(tiles, 0, dim)
+    shape = tiles.shape
+    return tiles.reshape(*shape[:dim], shape[dim] * shape[dim + 1], *shape[dim + 2 :])
+
+
+def sent_to_each(shard, axis, split_dim, concat_dim):
+    peers, index = (lax.axis_size(axis), lax.axis_index(axis))
+    parts = cut_along(shard, split_dim, peers)
+    filled = parts
+    for lap in range(1, peers):
+        target, source = ((index + lap) % peers, (index - lap) % peers)
+        sent = lax.dynamic_index_in_dim(parts, target, 0)
+        other = lax.ppermute(sent, axis, [(i, (i + lap) % peers) for i in range(peers)])
+        filled = lax.dynamic_update_slice_in_dim(filled, other, source, axis=0)
+    return in_order(filled, concat_dim)
 
 
 def with_halo(cells, sides, width):
@@ -100,7 +123,7 @@
     )
     arrived, arrived_tags = (
         lax.all_to_all(outgoing, "seq", split_axis=0, concat_axis=0, tiled=True),
-        lax.all_to_all(labels, "seq", split_axis=0, concat_axis=0, tiled=True),
+        sent_to_each(labels, "seq", 0, 0),
     )
     x0 = arrived.reshape(slots, LAT).astype(jnp.float32)
     tag = arrived_tags.reshape(slots).astype(jnp.float32)

time: 211 us -> 239 us (1.13)
  starting transfers between devices: 19 us -> 36.3 us
  local copies, waits for them, and re-layouts: 21.4 us -> 32.4 us
    ppermute x0 -> x15, starting transfers between devices: none -> 26.8 us  [sent_to_each(): lax.ppermute(sent, axis, [(i, (i + lap) % peers) for i in range(peers)])]
    dynamic_update_slice x0 -> x15, local copies, waits for them, and re-layouts: none -> 9.58 us  [sent_to_each(): filled = lax.dynamic_update_slice_in_dim(filled, other, source, axis=0)]
    all_to_all x1 -> x0, starting transfers between devices: 8.62 us -> none  [per_device(): lax.all_to_all(labels, 'seq', split_axis=0, concat_axis=0, tiled=True)]
    unnamed x59 -> x57, local copies, waits for them, and re-layouts: 7.35 us -> 7.35 us
  transfers between devices with their start and end apart: 5 -> 19, of which waited for: 2 -> 2; matrix products, arithmetic and copies ran while one was open for 7% -> 11% of each run, Pallas kernels for 0% -> 0%
where the time goes in v1:
time: 239 us
  waiting for transfers between devices  104 us (44%)
  starting transfers between devices  36.3 us (15%)
  local copies, waits for them, and re-layouts  32.4 us (14%)
  blocking collectives  30.2 us (13%)
  between operations  14.8 us (6%)
  other arithmetic  10.9 us (5%)
  matrix products  10.4 us (4%)
    psum x1, waiting for transfers between devices, per_device(): summed = lax.psum(grad_part, ('dp', 'seq'))  96.9 us
    psum x1, blocking collectives, per_device(): clip_loss = lax.psum(partial_loss, 'seq').reshape(1, CLIPS)  30.2 us
    ppermute x15, starting transfers between devices, sent_to_each(): lax.ppermute(sent, axis, [(i, (i + lap) % peers) for i in range(peers)])  26.8 us
    dynamic_update_slice x15, local copies, waits for them, and re-layouts, sent_to_each(): filled = lax.dynamic_update_slice_in_dim(filled, other, source, axis=0)  9.58 us
    unnamed x57, local copies, waits for them, and re-layouts  7.35 us
    all_to_all x1, waiting for transfers between devices, per_device(): lax.all_to_all(outgoing, 'seq', split_axis=0, concat_axis=0, tiled=True)  6.64 us
    dot_general x3, matrix products, conv_rows(): jnp.dot(columns, kernel[lag].reshape(9 * chans, chans), preferred_element...  6.34 us
    all_to_all x1, starting transfers between devices, per_device(): lax.all_to_all(outgoing, 'seq', split_axis=0, concat_axis=0, tiled=True)  5.18 us
  transfers between devices with their start and end apart: 19, of which 2 were waited for; matrix products, arithmetic and copies ran while one was open for 11% of the time, Pallas kernels for 0%

profile of v1, /device:TPU:0, one launch (start us, length us, event | category | flops | bytes accessed | tf_op | source)
XLA Modules:
  0.0 238.6 jit_solution(17347664633009379350)
XLA Ops:
  7.2 2.0 fusion.43
  9.2 3.1 %collective-permute-start = (bf16[1,16,1,48,128]{4,3,2,1,0:T(8,128)(2,1)}, bf16[1,16,1,48,128]{4,3,2,1,0:T(8,128)(2,1)}, u32[]{:S(2)}, u32[]{:S(2)}) collective-permute-start(bf16[1,16,1,48,128]{4,3,2,1,0:T(8,128)(2,1)} %get-tuple-element.17), channel_id=1, source_target_pairs={{0,1},{1,2},{2,3},{3,4},{4,5},{5,6},{6,7},{7,8},{8,9},{9,10},{10,1... | collective-permute-start | bytes 589832 | tf_op jit(solution)/shard_map/ppermute | solution.py:41
  18.9 2.6 %collective-permute-start.2 = (bf16[1,1,18]{2,0,1:T(2,128)(2,1)}, bf16[1,1,18]{2,0,1:T(2,128)(2,1)}, u32[]{:S(2)}, u32[]{:S(2)}) collective-permute-start(bf16[1,1,18]{2,0,1:T(2,128)(2,1)} %get-tuple-element.33), channel_id=1, source_target_pairs={{0,1},{1,2},{2,3},{3,4},{4,5},{5,6},{6,7},{7,8},{8,9},{9,10},{10,1... | collective-permute-start | bytes 116 | tf_op jit(solution)/shard_map/ppermute | solution.py:28
  21.5 1.7 collective-permute-start.3
  23.2 2.4 %collective-permute-start.4 = (bf16[1,1,18]{2,0,1:T(2,128)(2,1)}, bf16[1,1,18]{2,0,1:T(2,128)(2,1)}, u32[]{:S(2)}, u32[]{:S(2)}) collective-permute-start(bf16[1,1,18]{2,0,1:T(2,128)(2,1)} %get-tuple-element.31), channel_id=1, source_target_pairs={{0,3},{1,4},{2,5},{3,6},{4,7},{5,8},{6,9},{7,10},{8,11},{9,12},{10... | collective-permute-start | bytes 116 | tf_op jit(solution)/shard_map/ppermute | solution.py:28
  26.3 2.8 %copy.30 = f32[1,16,4,48,128]{4,1,3,2,0:T(8,128)} copy(bf16[1,16,4,48,128]{4,3,2,1,0:T(8,128)(2,1)} %param.11) | data formatting | bytes 2359296 | tf_op jit(solution)/shard_map/convert_element_type | solution.py:98
  29.0 2.1 fusion.42
  35.1 1.6 collective-permute-start.5
  38.7 1.6 collective-permute-start.7
  40.9 4.4 %collective-permute-start.8 = (bf16[1,1,18]{2,0,1:T(2,128)(2,1)}, bf16[1,1,18]{2,0,1:T(2,128)(2,1)}, u32[]{:S(2)}, u32[]{:S(2)}) collective-permute-start(bf16[1,1,18]{2,0,1:T(2,128)(2,1)} %get-tuple-element.27), channel_id=1, source_target_pairs={{0,7},{1,8},{2,9},{3,10},{4,11},{5,12},{6,13},{7,14},{8,15},{9,0},... | collective-permute-start | bytes 116 | tf_op jit(solution)/shard_map/ppermute | solution.py:28
  48.0 2.1 collective-permute-start.11
  50.7 2.4 %collective-permute-start.12 = (bf16[1,1,18]{2,0,1:T(2,128)(2,1)}, bf16[1,1,18]{2,0,1:T(2,128)(2,1)}, u32[]{:S(2)}, u32[]{:S(2)}) collective-permute-start(bf16[1,1,18]{2,0,1:T(2,128)(2,1)} %get-tuple-element.23), channel_id=1, source_target_pairs={{0,11},{1,12},{2,13},{3,14},{4,15},{5,0},{6,1},{7,2},{8,3},{9,4},{... | collective-permute-start | bytes 116 | tf_op jit(solution)/shard_map/ppermute | solution.py:28
  53.8 1.9 collective-permute-start.13
  57.0 2.2 collective-permute-start.15
  59.8 2.3 collective-permute-start.16
  74.9 2.0 fusion.45
  76.9 2.3 fusion.44
  79.2 2.1 multiply_add_fusion
  85.0 1.5 convolution_convert_fusion.1
  87.7 5.2 %all-to-all-start = ((bf16[16,2,576]{2,1,0:T(2,128)(2,1)}), bf16[16,2,576]{2,1,0:T(2,128)(2,1)S(1)}, u32[]{:S(2)}, u32[]{:S(2)}) async-start(bf16[16,2,576]{2,1,0:T(2,128)(2,1)} %reshape.223), calls=%async_computation | async-start | bytes 81920 | tf_op jit(solution)/shard_map/all_to_all | solution.py:125
  92.9 6.6 %all-to-all-done = bf16[16,2,576]{2,1,0:T(2,128)(2,1)S(1)} async-done(((bf16[16,2,576]{2,1,0:T(2,128)(2,1)}), bf16[16,2,576]{2,1,0:T(2,128)(2,1)S(1)}, u32[]{:S(2)}, u32[]{:S(2)}) %all-to-all-start) | async-done | bytes 36896 | tf_op jit(solution)/shard_map/all_to_all | solution.py:125
  103.1 30.2 %psum.14 = f32[1,4]{1,0:T(1,128)} all-reduce(f32[1,4]{1,0:T(1,128)S(1)} %multiply_bitcast_fusion), channel_id=1, replica_groups=mesh['dp'=2,'seq'=16] {'seq'}, use_global_device_ids=true, to_apply=%region_11.12 | all-reduce | flops 4 | bytes 32 | tf_op jit(solution)/shard_map/psum | solution.py:151
  133.3 96.9 %all-reduce.4.cloned.1.call-done = f32[3072,64]{0,1:T(8,128)} async-done(((f32[3072,64]{0,1:T(8,128)}), f32[3072,64]{0,1:T(8,128)}) %all-reduce.4.cloned.1.call-update) | async-done | bytes 786448 | tf_op jit(solution)/shard_map/psum | solution.py:157
  230.2 1.6 constant_dynamic-slice_fusion
  (147 shorter events, 40.3 us)
Async XLA Ops:
  7.2 92.7 %copy-start = (bf16[3072,64]{0,1:T(8,128)(2,1)S(1)}, bf16[3072,64]{0,1:T(8,128)(2,1)}, u32[]{:S(2)}) copy-start(bf16[3072,64]{0,1:T(8,128)(2,1)} %param.21) | copy-start | bytes 1179652
  7.2 24.5 %copy-start.16 = (s32[1,4]{1,0:T(1,128)S(1)}, s32[1,4]{1,0:T(1,128)}, u32[]{:S(2)}) copy-start(s32[1,4]{1,0:T(1,128)} %param.13) | copy-start | bytes 52
  7.2 25.0 %copy-start.1 = (bf16[1,288,3072]{2,1,0:T(8,128)(2,1)S(1)}, bf16[1,288,3072]{2,1,0:T(8,128)(2,1)}, u32[]{:S(2)}) copy-start(bf16[1,288,3072]{2,1,0:T(8,128)(2,1)} %param.18) | copy-start | bytes 5308420
  9.2 56.5 %collective-permute-start = (bf16[1,16,1,48,128]{4,3,2,1,0:T(8,128)(2,1)}, bf16[1,16,1,48,128]{4,3,2,1,0:T(8,128)(2,1)}, u32[]{:S(2)}, u32[]{:S(2)}) collective-permute-start(bf16[1,16,1,48,128]{4,3,2,1,0:T(8,128)(2,1)} %get-tuple-element.17), channel_id=1, source_target_pairs={{0,1},{1,2},{2,3},{3,4},{4,5},{5,6},{6,7},{7,8},{8,9},{9,10},{10,1... | collective-permute-start | bytes 589832 | tf_op jit(solution)/shard_map/ppermute | solution.py:41
  12.2 53.4 %collective-permute-start.1 = (bf16[1,16,1,48,128]{4,3,2,1,0:T(8,128)(2,1)}, bf16[1,16,1,48,128]{4,3,2,1,0:T(8,128)(2,1)}, u32[]{:S(2)}, u32[]{:S(2)}) collective-permute-start(bf16[1,16,1,48,128]{4,3,2,1,0:T(8,128)(2,1)} %get-tuple-element.18), channel_id=1, source_target_pairs={{1,0},{2,1},{3,2},{4,3},{5,4},{6,5},{7,6},{8,7},{9,8},{10,9},{11,1... | collective-permute-start | bytes 589832 | tf_op jit(solution)/shard_map/ppermute | solution.py:43
  18.9 16.3 %collective-permute-start.2 = (bf16[1,1,18]{2,0,1:T(2,128)(2,1)}, bf16[1,1,18]{2,0,1:T(2,128)(2,1)}, u32[]{:S(2)}, u32[]{:S(2)}) collective-permute-start(bf16[1,1,18]{2,0,1:T(2,128)(2,1)} %get-tuple-element.33), channel_id=1, source_target_pairs={{0,1},{1,2},{2,3},{3,4},{4,5},{5,6},{6,7},{7,8},{8,9},{9,10},{10,1... | collective-permute-start | bytes 116 | tf_op jit(solution)/shard_map/ppermute | solution.py:28
  21.5 15.8 %collective-permute-start.3 = (bf16[1,1,18]{2,0,1:T(2,128)(2,1)}, bf16[1,1,18]{2,0,1:T(2,128)(2,1)}, u32[]{:S(2)}, u32[]{:S(2)}) collective-permute-start(bf16[1,1,18]{2,0,1:T(2,128)(2,1)} %get-tuple-element.32), channel_id=1, source_target_pairs={{0,2},{1,3},{2,4},{3,5},{4,6},{5,7},{6,8},{7,9},{8,10},{9,11},{10,... | collective-permute-start | bytes 116 | tf_op jit(solution)/shard_map/ppermute | solution.py:28
  23.2 15.5 %collective-permute-start.4 = (bf16[1,1,18]{2,0,1:T(2,128)(2,1)}, bf16[1,1,18]{2,0,1:T(2,128)(2,1)}, u32[]{:S(2)}, u32[]{:S(2)}) collective-permute-start(bf16[1,1,18]{2,0,1:T(2,128)(2,1)} %get-tuple-element.31), channel_id=1, source_target_pairs={{0,3},{1,4},{2,5},{3,6},{4,7},{5,8},{6,9},{7,10},{8,11},{9,12},{10... | collective-permute-start | bytes 116 | tf_op jit(solution)/shard_map/ppermute | solution.py:28
  32.2 33.4 %copy-start.4 = (bf16[1,16,4,48,128]{4,3,2,1,0:T(8,128)(2,1)S(1)}, bf16[1,16,4,48,128]{4,3,2,1,0:T(8,128)(2,1)}, u32[]{:S(2)}) copy-start(bf16[1,16,4,48,128]{4,3,2,1,0:T(8,128)(2,1)} %param.11) | copy-start | bytes 2359300
  35.1 5.8 %collective-permute-start.5 = (bf16[1,1,18]{2,0,1:T(2,128)(2,1)}, bf16[1,1,18]{2,0,1:T(2,128)(2,1)}, u32[]{:S(2)}, u32[]{:S(2)}) collective-permute-start(bf16[1,1,18]{2,0,1:T(2,128)(2,1)} %get-tuple-element.30), channel_id=1, source_target_pairs={{0,4},{1,5},{2,6},{3,7},{4,8},{5,9},{6,10},{7,11},{8,12},{9,13},{1... | collective-permute-start | bytes 116 | tf_op jit(solution)/shard_map/ppermute | solution.py:28
  37.3 8.6 %collective-permute-start.6 = (bf16[1,1,18]{2,0,1:T(2,128)(2,1)}, bf16[1,1,18]{2,0,1:T(2,128)(2,1)}, u32[]{:S(2)}, u32[]{:S(2)}) collective-permute-start(bf16[1,1,18]{2,0,1:T(2,128)(2,1)} %get-tuple-element.29), channel_id=1, source_target_pairs={{0,5},{1,6},{2,7},{3,8},{4,9},{5,10},{6,11},{7,12},{8,13},{9,14},{... | collective-permute-start | bytes 116 | tf_op jit(solution)/shard_map/ppermute | solution.py:28
  38.7 8.3 %collective-permute-start.7 = (bf16[1,1,18]{2,0,1:T(2,128)(2,1)}, bf16[1,1,18]{2,0,1:T(2,128)(2,1)}, u32[]{:S(2)}, u32[]{:S(2)}) collective-permute-start(bf16[1,1,18]{2,0,1:T(2,128)(2,1)} %get-tuple-element.28), channel_id=1, source_target_pairs={{0,6},{1,7},{2,8},{3,9},{4,10},{5,11},{6,12},{7,13},{8,14},{9,15},... | collective-permute-start | bytes 116 | tf_op jit(solution)/shard_map/ppermute | solution.py:28
  40.9 7.0 %collective-permute-start.8 = (bf16[1,1,18]{2,0,1:T(2,128)(2,1)}, bf16[1,1,18]{2,0,1:T(2,128)(2,1)}, u32[]{:S(2)}, u32[]{:S(2)}) collective-permute-start(bf16[1,1,18]{2,0,1:T(2,128)(2,1)} %get-tuple-element.27), channel_id=1, source_target_pairs={{0,7},{1,8},{2,9},{3,10},{4,11},{5,12},{6,13},{7,14},{8,15},{9,0},... | collective-permute-start | bytes 116 | tf_op jit(solution)/shard_map/ppermute | solution.py:28
  45.9 4.7 %collective-permute-start.9 = (bf16[1,1,18]{2,0,1:T(2,128)(2,1)}, bf16[1,1,18]{2,0,1:T(2,128)(2,1)}, u32[]{:S(2)}, u32[]{:S(2)}) collective-permute-start(bf16[1,1,18]{2,0,1:T(2,128)(2,1)} %get-tuple-element.26), channel_id=1, source_target_pairs={{0,8},{1,9},{2,10},{3,11},{4,12},{5,13},{6,14},{7,15},{8,0},{9,1},... | collective-permute-start | bytes 116 | tf_op jit(solution)/shard_map/ppermute | solution.py:28
  46.9 6.8 %collective-permute-start.10 = (bf16[1,1,18]{2,0,1:T(2,128)(2,1)}, bf16[1,1,18]{2,0,1:T(2,128)(2,1)}, u32[]{:S(2)}, u32[]{:S(2)}) collective-permute-start(bf16[1,1,18]{2,0,1:T(2,128)(2,1)} %get-tuple-element.25), channel_id=1, source_target_pairs={{0,9},{1,10},{2,11},{3,12},{4,13},{5,14},{6,15},{7,0},{8,1},{9,2},... | collective-permute-start | bytes 116 | tf_op jit(solution)/shard_map/ppermute | solution.py:28
  48.0 8.4 %collective-permute-start.11 = (bf16[1,1,18]{2,0,1:T(2,128)(2,1)}, bf16[1,1,18]{2,0,1:T(2,128)(2,1)}, u32[]{:S(2)}, u32[]{:S(2)}) collective-permute-start(bf16[1,1,18]{2,0,1:T(2,128)(2,1)} %get-tuple-element.24), channel_id=1, source_target_pairs={{0,10},{1,11},{2,12},{3,13},{4,14},{5,15},{6,0},{7,1},{8,2},{9,3},... | collective-permute-start | bytes 116 | tf_op jit(solution)/shard_map/ppermute | solution.py:28
  50.7 6.3 %collective-permute-start.12 = (bf16[1,1,18]{2,0,1:T(2,128)(2,1)}, bf16[1,1,18]{2,0,1:T(2,128)(2,1)}, u32[]{:S(2)}, u32[]{:S(2)}) collective-permute-start(bf16[1,1,18]{2,0,1:T(2,128)(2,1)} %get-tuple-element.23), channel_id=1, source_target_pairs={{0,11},{1,12},{2,13},{3,14},{4,15},{5,0},{6,1},{7,2},{8,3},{9,4},{... | collective-permute-start | bytes 116 | tf_op jit(solution)/shard_map/ppermute | solution.py:28
  53.8 6.1 %collective-permute-start.13 = (bf16[1,1,18]{2,0,1:T(2,128)(2,1)}, bf16[1,1,18]{2,0,1:T(2,128)(2,1)}, u32[]{:S(2)}, u32[]{:S(2)}) collective-permute-start(bf16[1,1,18]{2,0,1:T(2,128)(2,1)} %get-tuple-element.22), channel_id=1, source_target_pairs={{0,12},{1,13},{2,14},{3,15},{4,0},{5,1},{6,2},{7,3},{8,4},{9,5},{1... | collective-permute-start | bytes 116 | tf_op jit(solution)/shard_map/ppermute | solution.py:28
  56.3 6.4 %collective-permute-start.14 = (bf16[1,1,18]{2,0,1:T(2,128)(2,1)}, bf16[1,1,18]{2,0,1:T(2,128)(2,1)}, u32[]{:S(2)}, u32[]{:S(2)}) collective-permute-start(bf16[1,1,18]{2,0,1:T(2,128)(2,1)} %get-tuple-element.21), channel_id=1, source_target_pairs={{0,13},{1,14},{2,15},{3,0},{4,1},{5,2},{6,3},{7,4},{8,5},{9,6},{10... | collective-permute-start | bytes 116 | tf_op jit(solution)/shard_map/ppermute | solution.py:28
  57.0 6.4 %collective-permute-start.15 = (bf16[1,1,18]{2,0,1:T(2,128)(2,1)}, bf16[1,1,18]{2,0,1:T(2,128)(2,1)}, u32[]{:S(2)}, u32[]{:S(2)}) collective-permute-start(bf16[1,1,18]{2,0,1:T(2,128)(2,1)} %get-tuple-element.20), channel_id=1, source_target_pairs={{0,14},{1,15},{2,0},{3,1},{4,2},{5,3},{6,4},{7,5},{8,6},{9,7},{10,... | collective-permute-start | bytes 116 | tf_op jit(solution)/shard_map/ppermute | solution.py:28
  59.8 4.3 %collective-permute-start.16 = (bf16[1,1,18]{2,0,1:T(2,128)(2,1)S(1)}, bf16[1,1,18]{2,0,1:T(2,128)(2,1)}, u32[]{:S(2)}, u32[]{:S(2)}) collective-permute-start(bf16[1,1,18]{2,0,1:T(2,128)(2,1)S(1)} %get-tuple-element.19), channel_id=1, source_target_pairs={{0,15},{1,0},{2,1},{3,2},{4,3},{5,4},{6,5},{7,6},{8,7},{9,8},{10,9... | collective-permute-start | bytes 116 | tf_op jit(solution)/shard_map/ppermute | solution.py:28
  83.1 16.7 %copy-start.7 = (f32[1,288,64]{1,2,0:T(8,128)S(1)}, f32[1,288,64]{1,2,0:T(8,128)}, u32[]{:S(2)}) copy-start(f32[1,288,64]{1,2,0:T(8,128)} %param.19) | copy-start | bytes 221188
  87.7 11.9 %all-to-all-start = ((bf16[16,2,576]{2,1,0:T(2,128)(2,1)}), bf16[16,2,576]{2,1,0:T(2,128)(2,1)S(1)}, u32[]{:S(2)}, u32[]{:S(2)}) async-start(bf16[16,2,576]{2,1,0:T(2,128)(2,1)} %reshape.223), calls=%async_computation | async-start | bytes 81920 | tf_op jit(solution)/shard_map/all_to_all | solution.py:125
  92.9 137.3 %all-reduce.4.cloned.1.call-start = ((), (), s32[]{:S(2)}) async-start(), calls=%async_computation.1 | async-start | bytes 1572864 | tf_op jit(solution)/shard_map/psum | solution.py:157
  (13 other events, 82.9 us)
Sparse Core Ops, SparseCore 0:
  102.4 127.7 all-reduce.3
